TPU v7x, 512 devices: a whole 4x8x8 slice. The times are simulated.
512 devices in a mesh: ctx: 64 (over y, x, core), head: 8 (over z).
Axes of the slice: x: 4, y: 8, z: 8, core: 2. Of those that a mesh axis runs over, the one named last changes fastest.
Arguments:
- tokens: bfloat16 [65536, 2048], P('ctx', 'head'), may hold values from -6 to 6
- w_qkv: bfloat16 [3, 2048, 2048], P(None, 'ctx', 'head'), may hold values from -0.125 to 0.125
- out_gain: float32 [2048], P('head'), may hold values from 0.25 to 1.75
- seg_ids: int32 [65536], P('ctx'), may hold values from 0 to 15, never falling along the last dimension, each value on 1 to 16384 neighbouring positions
Outputs:
- attended: bfloat16 [65536, 2048], P('ctx', 'head')
Inputs may be any that keep to these rules, and one draw needn't show every extreme that they name: `seg_ids`: segment numbers never fall along the stream; each segment covers 1 to 16384 consecutive tokens, and one covers exactly 16384.
All inputs are finite; a program needn't handle non-finite values.
Results may differ from a plain program's by a relative error of at most 0.012.
Values may be sent and summed in bfloat16 or wider, within the bound.
No kernel may reach another device: no remote copies, remote signals or barrier semaphores. Data moves between devices by JAX's collectives and lax.ppermute only.
A program may use at most 64 MiB of HBM per device.

v0:
```python
import jax
import jax.numpy as jnp
from jax import lax
from jax.sharding import Mesh
from jax.sharding import PartitionSpec as P

HEAD_DIM = 128
SPAN = 16384
CTX = ("y", "x", "core")


def shifted(value, axis, steps, count):
    return lax.ppermute(value, axis, [(source, source + steps) for source in range(count - steps)])


def ring_gather(value, axis, count, dim):
    by_offset = {0: value}
    ahead = value
    behind = value
    for step in range(1, count // 2 + 1):
        ahead = lax.ppermute(ahead, axis, [(j, (j + 1) % count) for j in range(count)])
        by_offset[-step] = ahead
        if step < count - count // 2:
            behind = lax.ppermute(behind, axis, [(j, (j - 1) % count) for j in range(count)])
            by_offset[step] = behind
    low = -(count // 2)
    stacked = jnp.stack([by_offset[off] for off in range(low, low + count)], axis=0)
    ordered = jnp.roll(stacked, lax.axis_index(axis) + low, axis=0)
    moved = jnp.moveaxis(ordered, 0, dim)
    shape = list(value.shape)
    shape[dim] *= count
    return moved.reshape(shape)


def gather_weights(w_local):
    half = w_local.shape[2] // 2
    core = lax.axis_index("core")
    partner = lax.ppermute(w_local, "core", [(0, 1), (1, 0)])
    low_rows = jnp.where(core == 0, w_local[:, :, :half], partner[:, :, half:])
    high_rows = jnp.where(core == 0, partner[:, :, :half], w_local[:, :, half:])
    rows = jnp.concatenate([low_rows, high_rows], axis=1)
    rows = direct_gather(rows, "x", lax.axis_size("x"), 1)
    rows = ring_gather(rows, "y", lax.axis_size("y"), 1)
    other = lax.ppermute(rows, "core", [(0, 1), (1, 0)])
    return jnp.where(
        core == 0, jnp.concatenate([rows, other], axis=2), jnp.concatenate([other, rows], axis=2)
    )


def direct_gather(value, axis, count, dim):
    low = -(count // 2)
    by_offset = {0: value}
    for off in range(low, low + count):
        if off != 0:
            by_offset[off] = lax.ppermute(
                value, axis, [(j, (j - off) % count) for j in range(count)]
            )
    stacked = jnp.stack([by_offset[off] for off in range(low, low + count)], axis=0)
    ordered = jnp.roll(stacked, lax.axis_index(axis) + low, axis=0)
    moved = jnp.moveaxis(ordered, 0, dim)
    shape = list(value.shape)
    shape[dim] *= count
    return moved.reshape(shape)


def feature_map(values):
    return (jax.nn.elu(values.astype(jnp.float32)) + 1.0).astype(jnp.bfloat16)


def state_scan(kv_state, tails, row_count):
    count = lax.axis_size(CTX)
    window = min(count - 1, 1 + (SPAN - 1) // row_count)
    row_len = lax.axis_size("x") * lax.axis_size("core")
    assert window <= 2 * row_len
    me = lax.axis_index(CTX)
    pos = me % row_len
    first = me - pos

    def tail_of(block):
        return jnp.where(block >= 0, tails[jnp.clip(block, 0, count - 1)], -1.0)

    prev_tail = tail_of(me - 1)
    spread = jnp.broadcast_to(kv_state.astype(jnp.bfloat16)[None], (row_len,) + kv_state.shape)
    row = lax.all_to_all(spread, ("x", "core"), 0, 0, tiled=True).astype(jnp.float32)
    places = jnp.arange(row_len)
    row_tails = tail_of(first + places)
    in_last = row_tails == row_tails[row_len - 1]

    def masked(mask):
        return jnp.sum(jnp.where(mask[:, None, None, None], row, 0.0), axis=0)

    y_count = lax.axis_size("y")
    one_back = shifted(masked(in_last).astype(jnp.bfloat16), "y", 1, y_count).astype(jnp.float32)
    two_back = shifted(
        masked(in_last & (places >= pos)).astype(jnp.bfloat16), "y", 2, y_count
    ).astype(jnp.float32)
    state = masked((places < pos) & (row_tails == prev_tail))
    state = state + jnp.where(tail_of(first - 1) == prev_tail, one_back, 0.0)
    if window > row_len:
        state = state + jnp.where(tail_of(first - row_len - 1) == prev_tail, two_back, 0.0)
    return (state, prev_tail)


def per_device(tokens, w_qkv, out_gain, seg_ids):
    whole = lax.all_gather(tokens, "head", axis=1, tiled=True)
    row_count = seg_ids.shape[0]
    groups = lax.axis_size(CTX)
    own_rows = w_qkv.shape[1]
    tail_row = jnp.full((w_qkv.shape[0], 1, w_qkv.shape[2]), seg_ids[-1], w_qkv.dtype)
    carried = gather_weights(jnp.concatenate([w_qkv, tail_row], axis=1))
    carried = carried.reshape(w_qkv.shape[0], groups, own_rows + 1, w_qkv.shape[2])
    w_rows = carried[:, :, :own_rows].reshape(w_qkv.shape[0], groups * own_rows, w_qkv.shape[2])
    tails = carried[0, :, own_rows, 0].astype(jnp.float32)
    key_value = jnp.einsum(
        "tr,grc->gtc", whole, w_rows[1:], preferred_element_type=jnp.float32
    ).astype(jnp.bfloat16)
    head_count = key_value.shape[2] // HEAD_DIM
    key_map = feature_map(key_value[0]).reshape(row_count, head_count, HEAD_DIM)
    values = key_value[1].reshape(row_count, head_count, HEAD_DIM)
    seg_float = seg_ids.astype(jnp.float32)
    tail_id = seg_float[-1]
    key_tail = jnp.where((seg_float == tail_id)[:, None, None], key_map, jnp.zeros_like(key_map))
    kv_state = jnp.einsum("thd,the->hde", key_tail, values, preferred_element_type=jnp.float32)
    tails, kv_state = lax.optimization_barrier((tails, kv_state))
    state_in, tail_in = state_scan(kv_state, tails, row_count)
    query_proj = jnp.einsum("tr,rc->tc", whole, w_rows[0], preferred_element_type=jnp.float32)
    query_proj = lax.reduce_precision(query_proj, exponent_bits=8, mantissa_bits=7)
    queries = feature_map(query_proj).reshape(row_count, head_count, HEAD_DIM)
    block_rows = min(512, row_count)
    pieces = []
    for blk_no in range(row_count // block_rows):
        first_row = blk_no * block_rows
        key_end = first_row + block_rows
        query_blk = queries[first_row:key_end]
        query_pos = first_row + jnp.arange(block_rows, dtype=jnp.int32)
        query_seg = seg_float[first_row:key_end]
        scores = jnp.einsum(
            "bhd,shd->hbs", query_blk, key_map[:key_end], preferred_element_type=jnp.float32
        )
        visible = (jnp.arange(key_end, dtype=jnp.int32)[None, :] <= query_pos[:, None]) & (
            seg_float[None, :key_end] == query_seg[:, None]
        )
        weights = jnp.where(visible[None], scores, 0.0).astype(jnp.bfloat16)
        pieces.append(
            jnp.einsum(
                "hbs,she->bhe", weights, values[:key_end], preferred_element_type=jnp.float32
            )
        )
    local_part = jnp.concatenate(pieces, axis=0)
    state_low = state_in.astype(jnp.bfloat16)
    prefix = jnp.einsum("thd,hde->the", queries, state_low, preferred_element_type=jnp.float32)
    prefix = jnp.where((seg_float == tail_in)[:, None, None], prefix, 0.0)
    numerator = local_part + prefix
    inv_norm = lax.rsqrt(jnp.mean(numerator * numerator, axis=-1, keepdims=True) + 1e-05)
    result = numerator * inv_norm * out_gain.reshape(head_count, HEAD_DIM)
    return result.astype(jnp.bfloat16).reshape(row_count, head_count * HEAD_DIM)


def solution(mesh):
    shape = dict(zip(mesh.axis_names, mesh.devices.shape))
    head = shape["head"]
    fine = Mesh(mesh.devices.reshape(-1, 4, 2, head), (*CTX, "head"))
    placed = (P(CTX, "head"), P(None, CTX, "head"), P("head"), P(CTX))
    return jax.shard_map(
        per_device, mesh=fine, in_specs=placed, out_specs=P(CTX, "head"), check_vma=False
    )
```

profile of v0, /device:TPU:18, one launch (start us, length us, event | category | flops | bytes accessed | tf_op | source)
XLA Modules:
  0.0 132.6 jit_solution(4561768235735514698)
XLA Ops:
  13.9 4.0 %collective-permute-start.1 = (bf16[3,66,128]{2,1,0:T(8,128)(2,1)S(1)}, bf16[3,66,128]{2,1,0:T(8,128)(2,1)S(1)}, u32[]{:S(2)}, u32[]{:S(2)}) collective-permute-start(bf16[3,66,128]{2,1,0:T(8,128)(2,1)S(1)} %pad_maximum_fusion), channel_id=1, source_target_pairs={{0,32},{16,48},{32,0},{48,16},{1,33},{17,49},{33,1},{49,17},{2,34}... | collective-permute-start | bytes 152072 | tf_op jit(solution)/shard_map/ppermute | solution.py:55
  18.0 1.9 %collective-permute-start.2 = (bf16[3,66,128]{2,1,0:T(8,128)(2,1)S(1)}, bf16[3,66,128]{2,1,0:T(8,128)(2,1)S(1)}, u32[]{:S(2)}, u32[]{:S(2)}) collective-permute-start(bf16[3,66,128]{2,1,0:T(8,128)(2,1)S(1)} %pad_maximum_fusion), channel_id=1, source_target_pairs={{0,16},{16,32},{32,48},{48,0},{1,17},{17,33},{33,49},{49,1},{2,18}... | collective-permute-start | bytes 152072 | tf_op jit(solution)/shard_map/ppermute | solution.py:55
  19.9 3.9 %collective-permute-start.3 = (bf16[3,66,128]{2,1,0:T(8,128)(2,1)S(1)}, bf16[3,66,128]{2,1,0:T(8,128)(2,1)S(1)}, u32[]{:S(2)}, u32[]{:S(2)}) collective-permute-start(bf16[3,66,128]{2,1,0:T(8,128)(2,1)S(1)} %pad_maximum_fusion), channel_id=1, source_target_pairs={{0,48},{16,0},{32,16},{48,32},{1,49},{17,1},{33,17},{49,33},{2,50}... | collective-permute-start | bytes 152072 | tf_op jit(solution)/shard_map/ppermute | solution.py:55
  26.2 3.5 %collective-permute-start.4 = (bf16[3,264,128]{2,1,0:T(8,128)(2,1)S(1)}, bf16[3,264,128]{2,1,0:T(8,128)(2,1)S(1)}, u32[]{:S(2)}, u32[]{:S(2)}) collective-permute-start(bf16[3,264,128]{2,1,0:T(8,128)(2,1)S(1)} %reshape.183), channel_id=1, source_target_pairs={{0,64},{64,128},{128,192},{192,256},{256,320},{320,384},{384,448},... | collective-permute-start | bytes 608264 | tf_op jit(solution)/shard_map/ppermute | solution.py:21
  29.7 4.1 %collective-permute-done.4 = bf16[3,264,128]{2,1,0:T(8,128)(2,1)S(1)} collective-permute-done((bf16[3,264,128]{2,1,0:T(8,128)(2,1)S(1)}, bf16[3,264,128]{2,1,0:T(8,128)(2,1)S(1)}, u32[]{:S(2)}, u32[]{:S(2)}) %collective-permute-start.4) | collective-permute-done | bytes 202784 | tf_op jit(solution)/shard_map/ppermute | solution.py:21
  33.9 3.8 %collective-permute-start.5 = (bf16[3,264,128]{2,1,0:T(8,128)(2,1)S(1)}, bf16[3,264,128]{2,1,0:T(8,128)(2,1)S(1)}, u32[]{:S(2)}, u32[]{:S(2)}) collective-permute-start(bf16[3,264,128]{2,1,0:T(8,128)(2,1)S(1)} %collective-permute-done.4), channel_id=1, source_target_pairs={{0,64},{64,128},{128,192},{192,256},{256,320},{320,384},{384,448},... | collective-permute-start | bytes 608264 | tf_op jit(solution)/shard_map/ppermute | solution.py:21
  37.6 4.2 %collective-permute-start.8 = (bf16[3,264,128]{2,1,0:T(8,128)(2,1)S(1)}, bf16[3,264,128]{2,1,0:T(8,128)(2,1)S(1)}, u32[]{:S(2)}, u32[]{:S(2)}) collective-permute-start(bf16[3,264,128]{2,1,0:T(8,128)(2,1)S(1)} %reshape.183), channel_id=1, source_target_pairs={{0,448},{64,0},{128,64},{192,128},{256,192},{320,256},{384,320},{4... | collective-permute-start | bytes 608264 | tf_op jit(solution)/shard_map/ppermute | solution.py:24
  43.6 2.9 %collective-permute-start.6 = (bf16[3,264,128]{2,1,0:T(8,128)(2,1)S(1)}, bf16[3,264,128]{2,1,0:T(8,128)(2,1)S(1)}, u32[]{:S(2)}, u32[]{:S(2)}) collective-permute-start(bf16[3,264,128]{2,1,0:T(8,128)(2,1)S(1)} %collective-permute-done.5), channel_id=1, source_target_pairs={{0,64},{64,128},{128,192},{192,256},{256,320},{320,384},{384,448},... | collective-permute-start | bytes 608264 | tf_op jit(solution)/shard_map/ppermute | solution.py:21
  46.9 3.7 %collective-permute-start.9 = (bf16[3,264,128]{2,1,0:T(8,128)(2,1)S(1)}, bf16[3,264,128]{2,1,0:T(8,128)(2,1)S(1)}, u32[]{:S(2)}, u32[]{:S(2)}) collective-permute-start(bf16[3,264,128]{2,1,0:T(8,128)(2,1)S(1)} %collective-permute-done.8), channel_id=1, source_target_pairs={{0,448},{64,0},{128,64},{192,128},{256,192},{320,256},{384,320},{4... | collective-permute-start | bytes 608264 | tf_op jit(solution)/shard_map/ppermute | solution.py:24
  52.4 2.9 %collective-permute-start.7 = (bf16[3,264,128]{2,1,0:T(8,128)(2,1)S(1)}, bf16[3,264,128]{2,1,0:T(8,128)(2,1)S(1)}, u32[]{:S(2)}, u32[]{:S(2)}) collective-permute-start(bf16[3,264,128]{2,1,0:T(8,128)(2,1)S(1)} %collective-permute-done.6), channel_id=1, source_target_pairs={{0,64},{64,128},{128,192},{192,256},{256,320},{320,384},{384,448},... | collective-permute-start | bytes 608264 | tf_op jit(solution)/shard_map/ppermute | solution.py:21
  55.8 3.8 %collective-permute-start.10 = (bf16[3,264,128]{2,1,0:T(8,128)(2,1)S(1)}, bf16[3,264,128]{2,1,0:T(8,128)(2,1)S(1)}, u32[]{:S(2)}, u32[]{:S(2)}) collective-permute-start(bf16[3,264,128]{2,1,0:T(8,128)(2,1)S(1)} %collective-permute-done.9), channel_id=1, source_target_pairs={{0,448},{64,0},{128,64},{192,128},{256,192},{320,256},{384,320},{4... | collective-permute-start | bytes 608264 | tf_op jit(solution)/shard_map/ppermute | solution.py:24
  61.5 3.2 %collective-permute-done.10 = bf16[3,264,128]{2,1,0:T(8,128)(2,1)S(1)} collective-permute-done((bf16[3,264,128]{2,1,0:T(8,128)(2,1)S(1)}, bf16[3,264,128]{2,1,0:T(8,128)(2,1)S(1)}, u32[]{:S(2)}, u32[]{:S(2)}) %collective-permute-start.10) | collective-permute-done | bytes 202784 | tf_op jit(solution)/shard_map/ppermute | solution.py:24
  66.5 1.9 %collective-permute-start.11 = (bf16[3,2112,128]{2,1,0:T(8,128)(2,1)}, bf16[3,2112,128]{2,1,0:T(8,128)(2,1)}, u32[]{:S(2)}, u32[]{:S(2)}) collective-permute-start(bf16[3,2112,128]{2,1,0:T(8,128)(2,1)} %bitcast.14), channel_id=1, source_target_pairs={{0,8},{8,0},{1,9},{9,1},{2,10},{10,2},{3,11},{11,3},{4,12},{12,4},... | collective-permute-start | bytes 4866056 | tf_op jit(solution)/shard_map/ppermute | solution.py:44
  72.1 2.5 %concatenate.35 = bf16[3,64,33,128]{3,2,1,0:T(8,128)(2,1)S(1)} reshape(bf16[3,8,264,128]{3,2,1,0:T(8,128)(2,1)} %copy.31) | data formatting | bytes 3244032 | tf_op jit(solution)/shard_map/concatenate | solution.py:46
  74.5 3.7 %concatenate.36 = bf16[3,64,33,128]{3,2,1,0:T(8,128)(2,1)} reshape(bf16[3,2112,128]{2,1,0:T(8,128)(2,1)} %collective-permute-done.11) | data formatting | bytes 3244032 | tf_op jit(solution)/shard_map/concatenate | solution.py:46
  78.2 2.8 %maximum_select_fusion = bf16[3,64,33,256]{3,2,1,0:T(8,128)(2,1)S(1)} fusion(bf16[3,64,33,128]{3,2,1,0:T(8,128)(2,1)} %concatenate.36, bf16[3,64,33,128]{3,2,1,0:T(8,128)(2,1)S(1)} %concatenate.35, pred[]{:T(512)S(6)} %eq.87), kind=kLoop, calls=%fused_computation.4 | loop fusion | flops 14598144 | bytes 6488065 | tf_op jit(solution)/shard_map/jit(_where)/select_n | solution.py:45
  83.0 4.1 %all-gather.2.cloned.1.call-done = bf16[1024,2048]{1,0:T(8,128)(2,1)} async-done(((bf16[1024,256]{1,0:T(8,128)(2,1)}), bf16[1024,2048]{1,0:T(8,128)(2,1)}) %all-gather.2.cloned.1.call-update) | async-done | bytes 4194320 | tf_op jit(solution)/shard_map/all_gather | solution.py:105
  87.2 4.6 %fusion.7 = bf16[2,1024,256]{1,2,0:T(8,128)(2,1)S(1)} fusion(bf16[2,2048,256]{2,1,0:T(8,128)(2,1)S(1)} %bitcast.97, bf16[1024,2048]{1,0:T(8,128)(2,1)} %all-gather.2.cloned.1.call-done), kind=kOutput, calls=%fused_computation.20 | convolution fusion | flops 2148007936 | bytes 7340032 | tf_op jit(solution)/shard_map/tr,grc->gtc/dot_general | solution.py:114
  94.3 4.8 %all-to-all-start = ((bf16[8,2,128,128]{3,2,1,0:T(8,128)(2,1)}), bf16[8,2,128,128]{3,2,1,0:T(8,128)(2,1)S(1)}, u32[]{:S(2)}, u32[]{:S(2)}) async-start(bf16[8,2,128,128]{3,2,1,0:T(8,128)(2,1)} %broadcast_in_dim.115), calls=%async_computation | async-start | bytes 1048576 | tf_op jit(solution)/shard_map/all_to_all | solution.py:84
  101.6 4.2 %fusion.21 = bf16[1024,256]{0,1:T(8,128)(2,1)S(1)} fusion(bf16[2048,256]{1,0:T(8,128)(2,1)} %bitcast.101, bf16[1024,2048]{1,0:T(8,128)(2,1)} %all-gather.2.cloned.1.call-done), kind=kOutput, calls=%fused_computation.34 | convolution fusion | flops 1075314688 | bytes 5767168 | tf_op jit(solution)/shard_map/tr,rc->tc/dot_general | solution.py:126
  109.3 2.8 %fusion.14 = f32[512,2,128]{0,2,1:T(8,128)S(1)} fusion(bf16[1024,2,128]{0,2,1:T(8,128)(2,1)} %bitcast.103, bf16[512,2,128]{0,2,1:T(8,128)(2,1)} %bitcast.106, pred[512,1024]{1,0:T(8,128)(4,1)} %fusion.2, f32[1024,2,128]{0,2,1:T(8,128)S(1)} %bitcast.100), kind=kOutput, calls=%fused_computation.27 | convolution fusion | flops 540278784 | bytes 2883584 | tf_op jit(solution)/shard_map/hbs,she->bhe/dot_general | solution.py:145
  112.5 5.5 %collective-permute-start.13 = (bf16[2,128,128]{2,1,0:T(8,128)(2,1)S(1)}, bf16[2,128,128]{2,1,0:T(8,128)(2,1)S(1)}, u32[]{:S(2)}, u32[]{:S(2)}) collective-permute-start(bf16[2,128,128]{2,1,0:T(8,128)(2,1)S(1)} %get-tuple-element.10), channel_id=1, source_target_pairs={{0,128},{64,192},{128,256},{192,320},{256,384},{320,448},{1,129},{... | collective-permute-start | bytes 196616 | tf_op jit(solution)/shard_map/ppermute | solution.py:13
  118.0 2.5 %collective-permute-start.12 = (bf16[2,128,128]{2,1,0:T(8,128)(2,1)S(1)}, bf16[2,128,128]{2,1,0:T(8,128)(2,1)S(1)}, u32[]{:S(2)}, u32[]{:S(2)}) collective-permute-start(bf16[2,128,128]{2,1,0:T(8,128)(2,1)S(1)} %get-tuple-element.9), channel_id=1, source_target_pairs={{0,64},{64,128},{128,192},{192,256},{256,320},{320,384},{384,448},... | collective-permute-start | bytes 196616 | tf_op jit(solution)/shard_map/ppermute | solution.py:13
  121.8 2.4 %collective-permute-done.12 = bf16[2,128,128]{2,1,0:T(8,128)(2,1)S(1)} collective-permute-done((bf16[2,128,128]{2,1,0:T(8,128)(2,1)S(1)}, bf16[2,128,128]{2,1,0:T(8,128)(2,1)S(1)}, u32[]{:S(2)}, u32[]{:S(2)}) %collective-permute-start.12) | collective-permute-done | bytes 65568 | tf_op jit(solution)/shard_map/ppermute | solution.py:13
  (85 shorter events, 33.0 us)
Async XLA Ops:
  6.5 80.7 %all-gather.2.cloned.1.call-start = ((), (), s32[]{:S(2)}) async-start(), calls=%async_computation.1 | async-start | bytes 4718592 | tf_op jit(solution)/shard_map/all_gather | solution.py:105
  9.3 3.1 %collective-permute-start = (bf16[3,33,256]{2,1,0:T(8,128)(2,1)S(1)}, bf16[3,33,256]{2,1,0:T(8,128)(2,1)S(1)}, u32[]{:S(2)}, u32[]{:S(2)}) collective-permute-start(bf16[3,33,256]{2,1,0:T(8,128)(2,1)S(1)} %concatenate.31), channel_id=1, source_target_pairs={{0,8},{8,0},{1,9},{9,1},{2,10},{10,2},{3,11},{11,3},{4,12},{12,4},... | collective-permute-start | bytes 152072 | tf_op jit(solution)/shard_map/ppermute | solution.py:38
  13.9 10.0 %collective-permute-start.1 = (bf16[3,66,128]{2,1,0:T(8,128)(2,1)S(1)}, bf16[3,66,128]{2,1,0:T(8,128)(2,1)S(1)}, u32[]{:S(2)}, u32[]{:S(2)}) collective-permute-start(bf16[3,66,128]{2,1,0:T(8,128)(2,1)S(1)} %pad_maximum_fusion), channel_id=1, source_target_pairs={{0,32},{16,48},{32,0},{48,16},{1,33},{17,49},{33,1},{49,17},{2,34}... | collective-permute-start | bytes 152072 | tf_op jit(solution)/shard_map/ppermute | solution.py:55
  18.0 6.0 %collective-permute-start.2 = (bf16[3,66,128]{2,1,0:T(8,128)(2,1)S(1)}, bf16[3,66,128]{2,1,0:T(8,128)(2,1)S(1)}, u32[]{:S(2)}, u32[]{:S(2)}) collective-permute-start(bf16[3,66,128]{2,1,0:T(8,128)(2,1)S(1)} %pad_maximum_fusion), channel_id=1, source_target_pairs={{0,16},{16,32},{32,48},{48,0},{1,17},{17,33},{33,49},{49,1},{2,18}... | collective-permute-start | bytes 152072 | tf_op jit(solution)/shard_map/ppermute | solution.py:55
  19.9 6.0 %collective-permute-start.3 = (bf16[3,66,128]{2,1,0:T(8,128)(2,1)S(1)}, bf16[3,66,128]{2,1,0:T(8,128)(2,1)S(1)}, u32[]{:S(2)}, u32[]{:S(2)}) collective-permute-start(bf16[3,66,128]{2,1,0:T(8,128)(2,1)S(1)} %pad_maximum_fusion), channel_id=1, source_target_pairs={{0,48},{16,0},{32,16},{48,32},{1,49},{17,1},{33,17},{49,33},{2,50}... | collective-permute-start | bytes 152072 | tf_op jit(solution)/shard_map/ppermute | solution.py:55
  26.2 7.6 %collective-permute-start.4 = (bf16[3,264,128]{2,1,0:T(8,128)(2,1)S(1)}, bf16[3,264,128]{2,1,0:T(8,128)(2,1)S(1)}, u32[]{:S(2)}, u32[]{:S(2)}) collective-permute-start(bf16[3,264,128]{2,1,0:T(8,128)(2,1)S(1)} %reshape.183), channel_id=1, source_target_pairs={{0,64},{64,128},{128,192},{192,256},{256,320},{320,384},{384,448},... | collective-permute-start | bytes 608264 | tf_op jit(solution)/shard_map/ppermute | solution.py:21
  33.9 9.7 %collective-permute-start.5 = (bf16[3,264,128]{2,1,0:T(8,128)(2,1)S(1)}, bf16[3,264,128]{2,1,0:T(8,128)(2,1)S(1)}, u32[]{:S(2)}, u32[]{:S(2)}) collective-permute-start(bf16[3,264,128]{2,1,0:T(8,128)(2,1)S(1)} %collective-permute-done.4), channel_id=1, source_target_pairs={{0,64},{64,128},{128,192},{192,256},{256,320},{320,384},{384,448},... | collective-permute-start | bytes 608264 | tf_op jit(solution)/shard_map/ppermute | solution.py:21
  37.6 9.3 %collective-permute-start.8 = (bf16[3,264,128]{2,1,0:T(8,128)(2,1)S(1)}, bf16[3,264,128]{2,1,0:T(8,128)(2,1)S(1)}, u32[]{:S(2)}, u32[]{:S(2)}) collective-permute-start(bf16[3,264,128]{2,1,0:T(8,128)(2,1)S(1)} %reshape.183), channel_id=1, source_target_pairs={{0,448},{64,0},{128,64},{192,128},{256,192},{320,256},{384,320},{4... | collective-permute-start | bytes 608264 | tf_op jit(solution)/shard_map/ppermute | solution.py:24
  43.6 8.8 %collective-permute-start.6 = (bf16[3,264,128]{2,1,0:T(8,128)(2,1)S(1)}, bf16[3,264,128]{2,1,0:T(8,128)(2,1)S(1)}, u32[]{:S(2)}, u32[]{:S(2)}) collective-permute-start(bf16[3,264,128]{2,1,0:T(8,128)(2,1)S(1)} %collective-permute-done.5), channel_id=1, source_target_pairs={{0,64},{64,128},{128,192},{192,256},{256,320},{320,384},{384,448},... | collective-permute-start | bytes 608264 | tf_op jit(solution)/shard_map/ppermute | solution.py:21
  46.9 8.8 %collective-permute-start.9 = (bf16[3,264,128]{2,1,0:T(8,128)(2,1)S(1)}, bf16[3,264,128]{2,1,0:T(8,128)(2,1)S(1)}, u32[]{:S(2)}, u32[]{:S(2)}) collective-permute-start(bf16[3,264,128]{2,1,0:T(8,128)(2,1)S(1)} %collective-permute-done.8), channel_id=1, source_target_pairs={{0,448},{64,0},{128,64},{192,128},{256,192},{320,256},{384,320},{4... | collective-permute-start | bytes 608264 | tf_op jit(solution)/shard_map/ppermute | solution.py:24
  52.4 8.8 %collective-permute-start.7 = (bf16[3,264,128]{2,1,0:T(8,128)(2,1)S(1)}, bf16[3,264,128]{2,1,0:T(8,128)(2,1)S(1)}, u32[]{:S(2)}, u32[]{:S(2)}) collective-permute-start(bf16[3,264,128]{2,1,0:T(8,128)(2,1)S(1)} %collective-permute-done.6), channel_id=1, source_target_pairs={{0,64},{64,128},{128,192},{192,256},{256,320},{320,384},{384,448},... | collective-permute-start | bytes 608264 | tf_op jit(solution)/shard_map/ppermute | solution.py:21
  55.8 8.9 %collective-permute-start.10 = (bf16[3,264,128]{2,1,0:T(8,128)(2,1)S(1)}, bf16[3,264,128]{2,1,0:T(8,128)(2,1)S(1)}, u32[]{:S(2)}, u32[]{:S(2)}) collective-permute-start(bf16[3,264,128]{2,1,0:T(8,128)(2,1)S(1)} %collective-permute-done.9), channel_id=1, source_target_pairs={{0,448},{64,0},{128,64},{192,128},{256,192},{320,256},{384,320},{4... | collective-permute-start | bytes 608264 | tf_op jit(solution)/shard_map/ppermute | solution.py:24
  65.0 4.0 %copy-start.1 = (s32[1024]{0:T(1024)S(1)}, s32[1024]{0:T(1024)}, u32[]{:S(2)}) copy-start(s32[1024]{0:T(1024)} %param.7) | copy-start | bytes 12292
  66.5 8.0 %collective-permute-start.11 = (bf16[3,2112,128]{2,1,0:T(8,128)(2,1)}, bf16[3,2112,128]{2,1,0:T(8,128)(2,1)}, u32[]{:S(2)}, u32[]{:S(2)}) collective-permute-start(bf16[3,2112,128]{2,1,0:T(8,128)(2,1)} %bitcast.14), channel_id=1, source_target_pairs={{0,8},{8,0},{1,9},{9,1},{2,10},{10,2},{3,11},{11,3},{4,12},{12,4},... | collective-permute-start | bytes 4866056 | tf_op jit(solution)/shard_map/ppermute | solution.py:44
  92.0 2.3 %copy-start = (bf16[1,1024,256]{1,2,0:T(8,128)(2,1)}, bf16[1,1024,256]{1,2,0:T(8,128)(2,1)S(1)}, u32[]{:S(2)}) copy-start(bf16[1,1024,256]{1,2,0:T(8,128)(2,1)S(1)} %get-tuple-element.17) | copy-start | bytes 1572868
  94.3 17.9 %all-to-all-start = ((bf16[8,2,128,128]{3,2,1,0:T(8,128)(2,1)}), bf16[8,2,128,128]{3,2,1,0:T(8,128)(2,1)S(1)}, u32[]{:S(2)}, u32[]{:S(2)}) async-start(bf16[8,2,128,128]{3,2,1,0:T(8,128)(2,1)} %broadcast_in_dim.115), calls=%async_computation | async-start | bytes 1048576 | tf_op jit(solution)/shard_map/all_to_all | solution.py:84
  112.2 12.4 %copy-start.2 = (f32[256]{0:T(256)S(1)}, f32[256]{0:T(256)}, u32[]{:S(2)}) copy-start(f32[256]{0:T(256)} %param.6) | copy-start | bytes 3076
  112.5 9.3 %collective-permute-start.13 = (bf16[2,128,128]{2,1,0:T(8,128)(2,1)S(1)}, bf16[2,128,128]{2,1,0:T(8,128)(2,1)S(1)}, u32[]{:S(2)}, u32[]{:S(2)}) collective-permute-start(bf16[2,128,128]{2,1,0:T(8,128)(2,1)S(1)} %get-tuple-element.10), channel_id=1, source_target_pairs={{0,128},{64,192},{128,256},{192,320},{256,384},{320,448},{1,129},{... | collective-permute-start | bytes 196616 | tf_op jit(solution)/shard_map/ppermute | solution.py:13
  118.0 6.2 %collective-permute-start.12 = (bf16[2,128,128]{2,1,0:T(8,128)(2,1)S(1)}, bf16[2,128,128]{2,1,0:T(8,128)(2,1)S(1)}, u32[]{:S(2)}, u32[]{:S(2)}) collective-permute-start(bf16[2,128,128]{2,1,0:T(8,128)(2,1)S(1)} %get-tuple-element.9), channel_id=1, source_target_pairs={{0,64},{64,128},{128,192},{192,256},{256,320},{320,384},{384,448},... | collective-permute-start | bytes 196616 | tf_op jit(solution)/shard_map/ppermute | solution.py:13
Sparse Core Ops, SparseCore 0:
  18.1 69.0 all-gather.1
where the time goes:
time: 134 us; the launch traced here: 133 us
  starting transfers between devices  51.1 us (38%)
  waiting for transfers between devices  23.2 us (17%)
  local copies, waits for them, and re-layouts  17.8 us (13%)
  between operations  15.9 us (12%)
  matrix products  14.4 us (11%)
  other arithmetic  10.1 us (8%)
    ppermute x4, starting transfers between devices, ring_gather(): lax.ppermute(ahead, axis, [(j, (j + 1) % count) for j in range(count)])  13 us
    ppermute x3, starting transfers between devices, ring_gather(): lax.ppermute(behind, axis, [(j, (j - 1) % count) for j in range(count)])  11.6 us
    ppermute x3, starting transfers between devices, direct_gather(): lax.ppermute(value, axis, [(j, (j - off) % count) for j in range(count)])  9.88 us
    ppermute x4, waiting for transfers between devices, ring_gather(): lax.ppermute(ahead, axis, [(j, (j + 1) % count) for j in range(count)])  9.33 us
    ppermute x2, starting transfers between devices, shifted(): lax.ppermute(value, axis, [(source, source + steps) for source in range(c...  8.02 us
    concatenate x2, local copies, waits for them, and re-layouts, gather_weights(): jnp.concatenate([rows, other], axis=2)  6.16 us
    all_to_all x1, starting transfers between devices, state_scan(): lax.all_to_all(spread, ('x', 'core'), 0, 0, tiled=True).astype(jnp.float32)  4.78 us
    dot_general x2, matrix products, per_device(): jnp.einsum('hbs,she->bhe', weights, values[:key_end], preferred_element_t...  4.73 us
  transfers between devices with their start and end apart: 16, of which 12 were waited for; matrix products, arithmetic and copies ran while one was open for 22% of the time, Pallas kernels for 0%

commit v1 on v0

--- a/solution.py
+++ b/solution.py
@@ -102,7 +102,9 @@
 
 
 def per_device(tokens, w_qkv, out_gain, seg_ids):
-    whole = lax.all_gather(tokens, "head", axis=1, tiled=True)
+    whole = jnp.concatenate(
+        lax.all_to_all(jnp.stack([tokens] * lax.axis_size("head")), "head", 0, 0), axis=1
+    )
     row_count = seg_ids.shape[0]
     groups = lax.axis_size(CTX)
     own_rows = w_qkv.shape[1]

time: 134 us -> 180 us (1.34)
  waiting for transfers between devices: 23.2 us -> 51.1 us
  local copies, waits for them, and re-layouts: 17.8 us -> 39.8 us
  between operations: 15.9 us -> 2.55 us
  starting transfers between devices: 51.1 us -> 60.8 us
    all_to_all x0 -> x1, waiting for transfers between devices: none -> 31.1 us  [per_device(): lax.all_to_all(jnp.stack([tokens] * lax.axis_size('head')), 'head', 0, 0)]
    reshape x0 -> x3, local copies, waits for them, and re-layouts: none -> 18.7 us  [per_device(): jnp.concatenate(lax.all_to_all(jnp.stack([tokens] * lax.axis_size('head')...]
    all_to_all x0 -> x1, starting transfers between devices: none -> 10.3 us  [per_device(): lax.all_to_all(jnp.stack([tokens] * lax.axis_size('head')), 'head', 0, 0)]
    ppermute x3, starting transfers between devices: 11.6 us -> 5.87 us  [ring_gather(): lax.ppermute(behind, axis, [(j, (j - 1) % count) for j in range(count)])]
    ppermute x4, starting transfers between devices: 13 us -> 17.8 us  [ring_gather(): lax.ppermute(ahead, axis, [(j, (j + 1) % count) for j in range(count)])]
    all_gather x1 -> x0, waiting for transfers between devices: 4.14 us -> none  [per_device(): whole = lax.all_gather(tokens, 'head', axis=1, tiled=True)]
    another operation x0 -> x1, local copies, waits for them, and re-layouts: none -> 3.29 us  [per_device(): jnp.stack([tokens] * lax.axis_size('head'))]
    ppermute x3, waiting for transfers between devices: 4.11 us -> 6.81 us  [ring_gather(): lax.ppermute(behind, axis, [(j, (j - 1) % count) for j in range(count)])]
  transfers between devices with their start and end apart: 16 -> 16, of which waited for: 12 -> 12; matrix products, arithmetic and copies ran while one was open for 22% -> 18% of each run, Pallas kernels for 0% -> 0%
where the time goes in v1:
time: 180 us; the launch traced here: 179 us
  starting transfers between devices  60.8 us (34%)
  waiting for transfers between devices  51.1 us (28%)
  local copies, waits for them, and re-layouts  39.8 us (22%)
  matrix products  14.5 us (8%)
  other arithmetic  10.2 us (6%)
  between operations  2.55 us (1%)
    all_to_all x1, waiting for transfers between devices, per_device(): lax.all_to_all(jnp.stack([tokens] * lax.axis_size('head')), 'head', 0, 0)  31.1 us
    reshape x3, local copies, waits for them, and re-layouts, per_device(): jnp.concatenate(lax.all_to_all(jnp.stack([tokens] * lax.axis_size('head')...  18.7 us
    ppermute x4, starting transfers between devices, ring_gather(): lax.ppermute(ahead, axis, [(j, (j + 1) % count) for j in range(count)])  17.8 us
    all_to_all x1, starting transfers between devices, per_device(): lax.all_to_all(jnp.stack([tokens] * lax.axis_size('head')), 'head', 0, 0)  10.3 us
    ppermute x3, starting transfers between devices, direct_gather(): lax.ppermute(value, axis, [(j, (j - off) % count) for j in range(count)])  9.86 us
    ppermute x2, starting transfers between devices, shifted(): lax.ppermute(value, axis, [(source, source + steps) for source in range(c...  8.3 us
    ppermute x4, waiting for transfers between devices, ring_gather(): lax.ppermute(ahead, axis, [(j, (j + 1) % count) for j in range(count)])  7.62 us
    ppermute x3, waiting for transfers between devices, ring_gather(): lax.ppermute(behind, axis, [(j, (j - 1) % count) for j in range(count)])  6.81 us
  transfers between devices with their start and end apart: 16, of which 12 were waited for; matrix products, arithmetic and copies ran while one was open for 18% of the time, Pallas kernels for 0%

profile of v1, /device:TPU:18, one launch (start us, length us, event | category | flops | bytes accessed | tf_op | source)
XLA Modules:
  0.0 178.9 jit_solution(15855963912923644055)
XLA Ops:
  7.4 4.0 %collective-permute-start.1 = (bf16[3,66,128]{2,1,0:T(8,128)(2,1)S(1)}, bf16[3,66,128]{2,1,0:T(8,128)(2,1)S(1)}, u32[]{:S(2)}, u32[]{:S(2)}) collective-permute-start(bf16[3,66,128]{2,1,0:T(8,128)(2,1)S(1)} %pad_maximum_fusion), channel_id=1, source_target_pairs={{0,32},{16,48},{32,0},{48,16},{1,33},{17,49},{33,1},{49,17},{2,34}... | collective-permute-start | bytes 152072 | tf_op jit(solution)/shard_map/ppermute | solution.py:55
  11.4 3.3 %stack.57 = bf16[8,1024,256]{2,1,0:T(8,128)(2,1)} broadcast(bf16[1024,256]{1,0:T(8,128)(2,1)} %param.4), dimensions={1,2} | broadcast | bytes 4718592 | tf_op jit(solution)/shard_map/stack | solution.py:106
  14.7 10.3 %all-to-all-start = ((bf16[8,1024,256]{2,1,0:T(8,128)(2,1)}), bf16[8,1024,256]{2,1,0:T(8,128)(2,1)}, u32[]{:S(2)}, u32[]{:S(2)}) async-start(bf16[8,1024,256]{2,1,0:T(8,128)(2,1)} %stack.57), calls=%async_computation | async-start | bytes 8388608 | tf_op jit(solution)/shard_map/all_to_all | solution.py:106
  27.0 3.9 %collective-permute-start.3 = (bf16[3,66,128]{2,1,0:T(8,128)(2,1)S(1)}, bf16[3,66,128]{2,1,0:T(8,128)(2,1)S(1)}, u32[]{:S(2)}, u32[]{:S(2)}) collective-permute-start(bf16[3,66,128]{2,1,0:T(8,128)(2,1)S(1)} %pad_maximum_fusion), channel_id=1, source_target_pairs={{0,48},{16,0},{32,16},{48,32},{1,49},{17,1},{33,17},{49,33},{2,50}... | collective-permute-start | bytes 152072 | tf_op jit(solution)/shard_map/ppermute | solution.py:55
  33.2 3.5 %collective-permute-start.4 = (bf16[3,264,128]{2,1,0:T(8,128)(2,1)S(1)}, bf16[3,264,128]{2,1,0:T(8,128)(2,1)S(1)}, u32[]{:S(2)}, u32[]{:S(2)}) collective-permute-start(bf16[3,264,128]{2,1,0:T(8,128)(2,1)S(1)} %reshape.191), channel_id=1, source_target_pairs={{0,64},{64,128},{128,192},{192,256},{256,320},{320,384},{384,448},... | collective-permute-start | bytes 608264 | tf_op jit(solution)/shard_map/ppermute | solution.py:21
  36.7 4.2 %collective-permute-done.4 = bf16[3,264,128]{2,1,0:T(8,128)(2,1)S(1)} collective-permute-done((bf16[3,264,128]{2,1,0:T(8,128)(2,1)S(1)}, bf16[3,264,128]{2,1,0:T(8,128)(2,1)S(1)}, u32[]{:S(2)}, u32[]{:S(2)}) %collective-permute-start.4) | collective-permute-done | bytes 202784 | tf_op jit(solution)/shard_map/ppermute | solution.py:21
  40.9 3.8 %collective-permute-start.5 = (bf16[3,264,128]{2,1,0:T(8,128)(2,1)S(1)}, bf16[3,264,128]{2,1,0:T(8,128)(2,1)S(1)}, u32[]{:S(2)}, u32[]{:S(2)}) collective-permute-start(bf16[3,264,128]{2,1,0:T(8,128)(2,1)S(1)} %collective-permute-done.4), channel_id=1, source_target_pairs={{0,64},{64,128},{128,192},{192,256},{256,320},{320,384},{384,448},... | collective-permute-start | bytes 608264 | tf_op jit(solution)/shard_map/ppermute | solution.py:21
  48.5 5.0 %collective-permute-start.6 = (bf16[3,264,128]{2,1,0:T(8,128)(2,1)S(1)}, bf16[3,264,128]{2,1,0:T(8,128)(2,1)S(1)}, u32[]{:S(2)}, u32[]{:S(2)}) collective-permute-start(bf16[3,264,128]{2,1,0:T(8,128)(2,1)S(1)} %collective-permute-done.5), channel_id=1, source_target_pairs={{0,64},{64,128},{128,192},{192,256},{256,320},{320,384},{384,448},... | collective-permute-start | bytes 608264 | tf_op jit(solution)/shard_map/ppermute | solution.py:21
  56.8 5.6 %collective-permute-start.7 = (bf16[3,264,128]{2,1,0:T(8,128)(2,1)S(1)}, bf16[3,264,128]{2,1,0:T(8,128)(2,1)S(1)}, u32[]{:S(2)}, u32[]{:S(2)}) collective-permute-start(bf16[3,264,128]{2,1,0:T(8,128)(2,1)S(1)} %collective-permute-done.6), channel_id=1, source_target_pairs={{0,64},{64,128},{128,192},{192,256},{256,320},{320,384},{384,448},... | collective-permute-start | bytes 608264 | tf_op jit(solution)/shard_map/ppermute | solution.py:21
  65.8 5.9 %collective-permute-done.10 = bf16[3,264,128]{2,1,0:T(8,128)(2,1)S(1)} collective-permute-done((bf16[3,264,128]{2,1,0:T(8,128)(2,1)S(1)}, bf16[3,264,128]{2,1,0:T(8,128)(2,1)S(1)}, u32[]{:S(2)}, u32[]{:S(2)}) %collective-permute-start.10) | collective-permute-done | bytes 202784 | tf_op jit(solution)/shard_map/ppermute | solution.py:24
  79.1 2.5 %concatenate.35 = bf16[3,64,33,128]{3,2,1,0:T(8,128)(2,1)S(1)} reshape(bf16[3,8,264,128]{3,2,1,0:T(8,128)(2,1)} %copy.44) | data formatting | bytes 3244032 | tf_op jit(solution)/shard_map/concatenate | solution.py:46
  81.6 3.7 %concatenate.36 = bf16[3,64,33,128]{3,2,1,0:T(8,128)(2,1)} reshape(bf16[3,2112,128]{2,1,0:T(8,128)(2,1)} %collective-permute-done.11) | data formatting | bytes 3244032 | tf_op jit(solution)/shard_map/concatenate | solution.py:46
  85.2 2.9 %maximum_select_fusion = bf16[3,64,33,256]{3,2,1,0:T(8,128)(2,1)S(1)} fusion(bf16[3,64,33,128]{3,2,1,0:T(8,128)(2,1)} %concatenate.36, bf16[3,64,33,128]{3,2,1,0:T(8,128)(2,1)S(1)} %concatenate.35, pred[]{:T(512)S(6)} %eq.87), kind=kLoop, calls=%fused_computation.2 | loop fusion | flops 14598144 | bytes 6488065 | tf_op jit(solution)/shard_map/jit(_where)/select_n | solution.py:45
  90.2 31.1 %all-to-all-done = bf16[8,1024,256]{2,1,0:T(8,128)(2,1)} async-done(((bf16[8,1024,256]{2,1,0:T(8,128)(2,1)}), bf16[8,1024,256]{2,1,0:T(8,128)(2,1)}, u32[]{:S(2)}, u32[]{:S(2)}) %all-to-all-start) | async-done | bytes 4194336 | tf_op jit(solution)/shard_map/all_to_all | solution.py:106
  121.3 6.5 %copy.46 = bf16[1024,8,256]{2,1,0:T(8,128)(2,1)} copy(bf16[1024,8,256]{2,0,1:T(8,128)(2,1)} %bitcast.16) | data formatting | bytes 8388608 | tf_op jit(solution)/shard_map/reshape | solution.py:105
  127.9 7.4 %reshape.208 = bf16[1024,2048,1]{1,0,2:T(8,128)(2,1)} reshape(bf16[1024,8,256]{2,1,0:T(8,128)(2,1)} %copy.46) | data formatting | bytes 8388608 | tf_op jit(solution)/shard_map/reshape | solution.py:105
  135.3 4.6 %fusion.2 = bf16[2,1024,256]{1,2,0:T(8,128)(2,1)S(1)} fusion(bf16[2,2048,256]{2,1,0:T(8,128)(2,1)S(1)} %bitcast.95, bf16[1024,2048,1]{1,0,2:T(8,128)(2,1)} %reshape.208), kind=kOutput, calls=%fused_computation.18 | convolution fusion | flops 2148007936 | bytes 7340032 | tf_op jit(solution)/shard_map/tr,grc->gtc/dot_general | solution.py:116
  140.9 4.8 %copy.64 = bf16[8,128,8,256]{3,2,0,1:T(8,128)(2,1)} copy(bf16[8,128,8,256]{3,2,1,0:T(8,128)(2,1)} %bitcast.39) | data formatting | bytes 8388608 | tf_op jit(solution)/shard_map/reshape | solution.py:105
  147.1 4.8 %all-to-all-start.1 = ((bf16[8,2,128,128]{3,2,1,0:T(8,128)(2,1)}), bf16[8,2,128,128]{3,2,1,0:T(8,128)(2,1)S(1)}, u32[]{:S(2)}, u32[]{:S(2)}) async-start(bf16[8,2,128,128]{3,2,1,0:T(8,128)(2,1)} %broadcast_in_dim.115), calls=%async_computation.1 | async-start | bytes 1048576 | tf_op jit(solution)/shard_map/all_to_all | solution.py:84
  154.5 4.2 %fusion.14 = bf16[1024,256]{0,1:T(8,128)(2,1)S(1)} fusion(bf16[2048,256]{1,0:T(8,128)(2,1)} %bitcast.99, bf16[1024,2048]{1,0:T(8,128)(2,1)} %bitcast.93), kind=kOutput, calls=%fused_computation.32 | convolution fusion | flops 1075314688 | bytes 5767168 | tf_op jit(solution)/shard_map/tr,rc->tc/dot_general | solution.py:128
  162.3 2.9 %fusion.7 = f32[512,2,128]{0,2,1:T(8,128)S(1)} fusion(bf16[1024,2,128]{0,2,1:T(8,128)(2,1)} %bitcast.101, bf16[512,2,128]{0,2,1:T(8,128)(2,1)} %bitcast.104, pred[512,1024]{1,0:T(8,128)(4,1)} %fusion, f32[1024,2,128]{0,2,1:T(8,128)S(1)} %bitcast.98), kind=kOutput, calls=%fused_computation.25 | convolution fusion | flops 540278784 | bytes 2883584 | tf_op jit(solution)/shard_map/hbs,she->bhe/dot_general | solution.py:147
  165.5 5.7 %collective-permute-start.13 = (bf16[2,128,128]{2,1,0:T(8,128)(2,1)S(1)}, bf16[2,128,128]{2,1,0:T(8,128)(2,1)S(1)}, u32[]{:S(2)}, u32[]{:S(2)}) collective-permute-start(bf16[2,128,128]{2,1,0:T(8,128)(2,1)S(1)} %get-tuple-element.10), channel_id=1, source_target_pairs={{0,128},{64,192},{128,256},{192,320},{256,384},{320,448},{1,129},{... | collective-permute-start | bytes 196616 | tf_op jit(solution)/shard_map/ppermute | solution.py:13
  171.2 2.6 %collective-permute-start.12 = (bf16[2,128,128]{2,1,0:T(8,128)(2,1)S(1)}, bf16[2,128,128]{2,1,0:T(8,128)(2,1)S(1)}, u32[]{:S(2)}, u32[]{:S(2)}) collective-permute-start(bf16[2,128,128]{2,1,0:T(8,128)(2,1)S(1)} %get-tuple-element.9), channel_id=1, source_target_pairs={{0,64},{64,128},{128,192},{192,256},{256,320},{320,384},{384,448},... | collective-permute-start | bytes 196616 | tf_op jit(solution)/shard_map/ppermute | solution.py:13
  175.1 2.3 %collective-permute-done.12 = bf16[2,128,128]{2,1,0:T(8,128)(2,1)S(1)} collective-permute-done((bf16[2,128,128]{2,1,0:T(8,128)(2,1)S(1)}, bf16[2,128,128]{2,1,0:T(8,128)(2,1)S(1)}, u32[]{:S(2)}, u32[]{:S(2)}) %collective-permute-start.12) | collective-permute-done | bytes 65568 | tf_op jit(solution)/shard_map/ppermute | solution.py:13
  (88 shorter events, 40.9 us)
Async XLA Ops:
  2.8 3.1 %collective-permute-start = (bf16[3,33,256]{2,1,0:T(8,128)(2,1)S(1)}, bf16[3,33,256]{2,1,0:T(8,128)(2,1)S(1)}, u32[]{:S(2)}, u32[]{:S(2)}) collective-permute-start(bf16[3,33,256]{2,1,0:T(8,128)(2,1)S(1)} %concatenate.31), channel_id=1, source_target_pairs={{0,8},{8,0},{1,9},{9,1},{2,10},{10,2},{3,11},{11,3},{4,12},{12,4},... | collective-permute-start | bytes 152072 | tf_op jit(solution)/shard_map/ppermute | solution.py:38
  7.4 23.5 %collective-permute-start.1 = (bf16[3,66,128]{2,1,0:T(8,128)(2,1)S(1)}, bf16[3,66,128]{2,1,0:T(8,128)(2,1)S(1)}, u32[]{:S(2)}, u32[]{:S(2)}) collective-permute-start(bf16[3,66,128]{2,1,0:T(8,128)(2,1)S(1)} %pad_maximum_fusion), channel_id=1, source_target_pairs={{0,32},{16,48},{32,0},{48,16},{1,33},{17,49},{33,1},{49,17},{2,34}... | collective-permute-start | bytes 152072 | tf_op jit(solution)/shard_map/ppermute | solution.py:55
  14.7 106.6 %all-to-all-start = ((bf16[8,1024,256]{2,1,0:T(8,128)(2,1)}), bf16[8,1024,256]{2,1,0:T(8,128)(2,1)}, u32[]{:S(2)}, u32[]{:S(2)}) async-start(bf16[8,1024,256]{2,1,0:T(8,128)(2,1)} %stack.57), calls=%async_computation | async-start | bytes 8388608 | tf_op jit(solution)/shard_map/all_to_all | solution.py:106
  25.0 6.0 %collective-permute-start.2 = (bf16[3,66,128]{2,1,0:T(8,128)(2,1)S(1)}, bf16[3,66,128]{2,1,0:T(8,128)(2,1)S(1)}, u32[]{:S(2)}, u32[]{:S(2)}) collective-permute-start(bf16[3,66,128]{2,1,0:T(8,128)(2,1)S(1)} %pad_maximum_fusion), channel_id=1, source_target_pairs={{0,16},{16,32},{32,48},{48,0},{1,17},{17,33},{33,49},{49,1},{2,18}... | collective-permute-start | bytes 152072 | tf_op jit(solution)/shard_map/ppermute | solution.py:55
  27.0 6.0 %collective-permute-start.3 = (bf16[3,66,128]{2,1,0:T(8,128)(2,1)S(1)}, bf16[3,66,128]{2,1,0:T(8,128)(2,1)S(1)}, u32[]{:S(2)}, u32[]{:S(2)}) collective-permute-start(bf16[3,66,128]{2,1,0:T(8,128)(2,1)S(1)} %pad_maximum_fusion), channel_id=1, source_target_pairs={{0,48},{16,0},{32,16},{48,32},{1,49},{17,1},{33,17},{49,33},{2,50}... | collective-permute-start | bytes 152072 | tf_op jit(solution)/shard_map/ppermute | solution.py:55
  33.2 7.7 %collective-permute-start.4 = (bf16[3,264,128]{2,1,0:T(8,128)(2,1)S(1)}, bf16[3,264,128]{2,1,0:T(8,128)(2,1)S(1)}, u32[]{:S(2)}, u32[]{:S(2)}) collective-permute-start(bf16[3,264,128]{2,1,0:T(8,128)(2,1)S(1)} %reshape.191), channel_id=1, source_target_pairs={{0,64},{64,128},{128,192},{192,256},{256,320},{320,384},{384,448},... | collective-permute-start | bytes 608264 | tf_op jit(solution)/shard_map/ppermute | solution.py:21
  40.9 7.6 %collective-permute-start.5 = (bf16[3,264,128]{2,1,0:T(8,128)(2,1)S(1)}, bf16[3,264,128]{2,1,0:T(8,128)(2,1)S(1)}, u32[]{:S(2)}, u32[]{:S(2)}) collective-permute-start(bf16[3,264,128]{2,1,0:T(8,128)(2,1)S(1)} %collective-permute-done.4), channel_id=1, source_target_pairs={{0,64},{64,128},{128,192},{192,256},{256,320},{320,384},{384,448},... | collective-permute-start | bytes 608264 | tf_op jit(solution)/shard_map/ppermute | solution.py:21
  44.7 9.3 %collective-permute-start.8 = (bf16[3,264,128]{2,1,0:T(8,128)(2,1)S(1)}, bf16[3,264,128]{2,1,0:T(8,128)(2,1)S(1)}, u32[]{:S(2)}, u32[]{:S(2)}) collective-permute-start(bf16[3,264,128]{2,1,0:T(8,128)(2,1)S(1)} %reshape.191), channel_id=1, source_target_pairs={{0,448},{64,0},{128,64},{192,128},{256,192},{320,256},{384,320},{4... | collective-permute-start | bytes 608264 | tf_op jit(solution)/shard_map/ppermute | solution.py:24
  48.5 8.2 %collective-permute-start.6 = (bf16[3,264,128]{2,1,0:T(8,128)(2,1)S(1)}, bf16[3,264,128]{2,1,0:T(8,128)(2,1)S(1)}, u32[]{:S(2)}, u32[]{:S(2)}) collective-permute-start(bf16[3,264,128]{2,1,0:T(8,128)(2,1)S(1)} %collective-permute-done.5), channel_id=1, source_target_pairs={{0,64},{64,128},{128,192},{192,256},{256,320},{320,384},{384,448},... | collective-permute-start | bytes 608264 | tf_op jit(solution)/shard_map/ppermute | solution.py:21
  54.0 8.8 %collective-permute-start.9 = (bf16[3,264,128]{2,1,0:T(8,128)(2,1)S(1)}, bf16[3,264,128]{2,1,0:T(8,128)(2,1)S(1)}, u32[]{:S(2)}, u32[]{:S(2)}) collective-permute-start(bf16[3,264,128]{2,1,0:T(8,128)(2,1)S(1)} %collective-permute-done.8), channel_id=1, source_target_pairs={{0,448},{64,0},{128,64},{192,128},{256,192},{320,256},{384,320},{4... | collective-permute-start | bytes 608264 | tf_op jit(solution)/shard_map/ppermute | solution.py:24
  56.8 8.8 %collective-permute-start.7 = (bf16[3,264,128]{2,1,0:T(8,128)(2,1)S(1)}, bf16[3,264,128]{2,1,0:T(8,128)(2,1)S(1)}, u32[]{:S(2)}, u32[]{:S(2)}) collective-permute-start(bf16[3,264,128]{2,1,0:T(8,128)(2,1)S(1)} %collective-permute-done.6), channel_id=1, source_target_pairs={{0,64},{64,128},{128,192},{192,256},{256,320},{320,384},{384,448},... | collective-permute-start | bytes 608264 | tf_op jit(solution)/shard_map/ppermute | solution.py:21
  62.8 8.9 %collective-permute-start.10 = (bf16[3,264,128]{2,1,0:T(8,128)(2,1)S(1)}, bf16[3,264,128]{2,1,0:T(8,128)(2,1)S(1)}, u32[]{:S(2)}, u32[]{:S(2)}) collective-permute-start(bf16[3,264,128]{2,1,0:T(8,128)(2,1)S(1)} %collective-permute-done.9), channel_id=1, source_target_pairs={{0,448},{64,0},{128,64},{192,128},{256,192},{320,256},{384,320},{4... | collective-permute-start | bytes 608264 | tf_op jit(solution)/shard_map/ppermute | solution.py:24
  72.1 4.1 %copy-start.1 = (s32[1024]{0:T(1024)S(1)}, s32[1024]{0:T(1024)}, u32[]{:S(2)}) copy-start(s32[1024]{0:T(1024)} %param.7) | copy-start | bytes 12292
  73.6 7.9 %collective-permute-start.11 = (bf16[3,2112,128]{2,1,0:T(8,128)(2,1)}, bf16[3,2112,128]{2,1,0:T(8,128)(2,1)}, u32[]{:S(2)}, u32[]{:S(2)}) collective-permute-start(bf16[3,2112,128]{2,1,0:T(8,128)(2,1)} %bitcast.14), channel_id=1, source_target_pairs={{0,8},{8,0},{1,9},{9,1},{2,10},{10,2},{3,11},{11,3},{4,12},{12,4},... | collective-permute-start | bytes 4866056 | tf_op jit(solution)/shard_map/ppermute | solution.py:44
  140.1 5.5 %copy-start = (bf16[1,1024,256]{1,2,0:T(8,128)(2,1)}, bf16[1,1024,256]{1,2,0:T(8,128)(2,1)S(1)}, u32[]{:S(2)}) copy-start(bf16[1,1024,256]{1,2,0:T(8,128)(2,1)S(1)} %get-tuple-element.17) | copy-start | bytes 1572868
  147.1 18.0 %all-to-all-start.1 = ((bf16[8,2,128,128]{3,2,1,0:T(8,128)(2,1)}), bf16[8,2,128,128]{3,2,1,0:T(8,128)(2,1)S(1)}, u32[]{:S(2)}, u32[]{:S(2)}) async-start(bf16[8,2,128,128]{3,2,1,0:T(8,128)(2,1)} %broadcast_in_dim.115), calls=%async_computation.1 | async-start | bytes 1048576 | tf_op jit(solution)/shard_map/all_to_all | solution.py:84
  165.1 12.6 %copy-start.2 = (f32[256]{0:T(256)S(1)}, f32[256]{0:T(256)}, u32[]{:S(2)}) copy-start(f32[256]{0:T(256)} %param.6) | copy-start | bytes 3076
  165.5 9.6 %collective-permute-start.13 = (bf16[2,128,128]{2,1,0:T(8,128)(2,1)S(1)}, bf16[2,128,128]{2,1,0:T(8,128)(2,1)S(1)}, u32[]{:S(2)}, u32[]{:S(2)}) collective-permute-start(bf16[2,128,128]{2,1,0:T(8,128)(2,1)S(1)} %get-tuple-element.10), channel_id=1, source_target_pairs={{0,128},{64,192},{128,256},{192,320},{256,384},{320,448},{1,129},{... | collective-permute-start | bytes 196616 | tf_op jit(solution)/shard_map/ppermute | solution.py:13
  171.2 6.2 %collective-permute-start.12 = (bf16[2,128,128]{2,1,0:T(8,128)(2,1)S(1)}, bf16[2,128,128]{2,1,0:T(8,128)(2,1)S(1)}, u32[]{:S(2)}, u32[]{:S(2)}) collective-permute-start(bf16[2,128,128]{2,1,0:T(8,128)(2,1)S(1)} %get-tuple-element.9), channel_id=1, source_target_pairs={{0,64},{64,128},{128,192},{192,256},{256,320},{320,384},{384,448},... | collective-permute-start | bytes 196616 | tf_op jit(solution)/shard_map/ppermute | solution.py:13
